TPU v7x, 256 devices: a whole 4x4x8 slice. The times are simulated.
256 devices in a mesh: dp: 16 (over z, core), tensor: 16 (over y, x).
Axes of the slice: x: 4, y: 4, z: 8, core: 2. Of those that a mesh axis runs over, the one named last changes fastest.
Arguments:
- hidden_rows: bfloat16 [16384, 3584], P(('dp', 'tensor')), parts along dimension 0, may hold values from -48 to 48
- norm_gain: float32 [3584], replicated, may hold values from 0.5 to 2
- gate_weight: bfloat16 [9216, 3584], P('tensor'), may hold values from -0.09375 to 0.09375
- up_weight: bfloat16 [9216, 3584], P('tensor'), may hold values from -0.09375 to 0.09375
- down_weight: bfloat16 [9216, 3584], P('tensor'), may hold values from -0.0625 to 0.0625
- span_lengths: int32 [256], P('dp'), parts along dimension 0, may hold values from 1 to 64, 512 in all
Outputs:
- ffn_out: bfloat16 [16384, 3584], P(('dp', 'tensor')), parts along dimension 0
There are 16 independent parts, one for each index of `dp`. A program takes and returns all parts, laid end to end along the dimension named above; an argument that names none is the same for every part. Nothing has to cross between parts.
Inputs may be any that keep to these rules, and one draw needn't show every extreme that they name: `span_lengths`: the lengths of one part sum to exactly 512, and the largest is exactly 64.
All inputs are finite; a program needn't handle non-finite values.
Results may differ from a plain program's by a relative error of at most 0.0065.
Values may be sent and summed in bfloat16 or wider, within the bound.
No kernel may reach another device: no remote copies, remote signals or barrier semaphores. Data moves between devices by JAX's collectives and lax.ppermute only.
A program may use at most 128 MiB of HBM per device.

v0:
```python
import jax
import jax.numpy as jnp
from jax import lax
from jax.sharding import PartitionSpec as P


def shards(hidden_rows, norm_gain, gate_weight, up_weight, down_weight, span_lengths):
    capacity = hidden_rows.shape[0]
    own_rank = lax.axis_index("tensor")
    widened = hidden_rows.astype(jnp.float32)
    scale = lax.rsqrt(jnp.mean(widened * widened, axis=-1, keepdims=True) + 1e-06)
    normed = (widened * scale * norm_gain).astype(jnp.bfloat16)
    dims = (((1,), (1,)), ((), ()))
    block_rows = lax.all_gather(normed, "tensor", axis=0, tiled=True)
    gate_part = lax.dot_general(block_rows, gate_weight, dims, preferred_element_type=jnp.float32)
    up_part = lax.dot_general(block_rows, up_weight, dims, preferred_element_type=jnp.float32)
    activations = (jax.nn.silu(gate_part) * up_part).astype(jnp.bfloat16)
    summed = lax.psum_scatter(
        jnp.dot(activations, down_weight, preferred_element_type=jnp.float32),
        "tensor",
        scatter_dimension=0,
        tiled=True,
    )
    result = summed.astype(jnp.bfloat16)
    live_mask = jnp.arange(capacity, dtype=jnp.int32) < span_lengths[own_rank]
    return jnp.where(live_mask[:, None], result, jnp.zeros_like(result))


def solution(mesh):
    return jax.shard_map(
        shards,
        mesh=mesh,
        in_specs=(
            P(("dp", "tensor"), None),
            P(),
            P("tensor", None),
            P("tensor", None),
            P("tensor", None),
            P("dp"),
        ),
        out_specs=P(("dp", "tensor"), None),
        check_vma=False,
    )
```

profile of v0, /device:TPU:1, one launch (start us, length us, event | category | flops | bytes accessed | tf_op | source)
XLA Modules:
  0.0 225.9 jit_solution(6906171612249363775)
XLA Ops:
  6.5 0.0 all-gather.2.cloned.1.call-start
  6.5 1.2 fusion
  7.8 2.0 fusion.2
  9.7 0.0 all-gather.2.cloned.1.call-update
  9.8 0.0 reduce-scatter.2.cloned.1.call-start
  9.8 75.1 %all-gather.2.cloned.1.call-done = bf16[1024,3584]{1,0:T(8,128)(2,1)} async-done(((bf16[64,3584]{1,0:T(8,128)(2,1)}), bf16[1024,3584]{1,0:T(8,128)(2,1)}) %all-gather.2.cloned.1.call-update) | async-done | bytes 7340048 | tf_op jit(solution)/shard_map/all_gather | solution.py:14
  84.9 8.0 %fusion.3 = f32[1024,576]{0,1:T(8,128)S(1)} fusion(bf16[1024,3584]{1,0:T(8,128)(2,1)} %all-gather.2.cloned.1.call-done, bf16[576,3584]{1,0:T(8,128)(2,1)} %param.8), kind=kOutput, calls=%fused_computation.9 | convolution fusion | flops 4227858432 | bytes 13828096 | tf_op jit(solution)/shard_map/dot_general | solution.py:15
  92.8 18.1 %fusion.4 = f32[1024,3584]{1,0:T(8,128)} fusion(bf16[576,3584]{1,0:T(8,128)(2,1)} %param.10, f32[1024,576]{0,1:T(8,128)S(1)} %fusion.3, bf16[1024,3584]{1,0:T(8,128)(2,1)} %all-gather.2.cloned.1.call-done, bf16[576,3584]{1,0:T(8,128)(2,1)} %param.9), kind=kOutput, calls=%fused_computation.10 | convolution fusion | flops 8459255808 | bytes 32636928 | tf_op jit(solution)/shard_map/dot_general | solution.py:19
  111.0 0.0 copy-start
  111.0 0.0 reduce-scatter.2.cloned.1.call-update
  111.0 0.6 copy-done
  111.6 0.6 dynamic_slice.3
  112.2 0.6 iota_compare_fusion
  112.9 104.2 %reduce-scatter.2.cloned.1.call-done = f32[64,3584]{1,0:T(8,128)} async-done(((f32[1024,3584]{1,0:T(8,128)}), f32[64,3584]{1,0:T(8,128)}) %reduce-scatter.2.cloned.1.call-update) | async-done | bytes 917520 | tf_op jit(solution)/shard_map/reduce_scatter | solution.py:18
  217.0 2.1 convert_select_fusion
  (1 shorter events, 0.0 us)
Async XLA Ops:
  6.5 78.3 %all-gather.2.cloned.1.call-start = ((), (), s32[]{:S(2)}) async-start(), calls=%async_computation.1 | async-start | bytes 7798784 | tf_op jit(solution)/shard_map/all_gather | solution.py:14
  9.8 207.3 %reduce-scatter.2.cloned.1.call-start = ((), (), s32[]{:S(2)}) async-start(), calls=%async_computation.2 | async-start | bytes 15597568 | tf_op jit(solution)/shard_map/reduce_scatter | solution.py:18
  111.0 0.7 copy-start
Sparse Core Ops, SparseCore 0:
  9.9 74.9 all-gather.1
  111.1 105.8 reduce-scatter.1
where the time goes:
time: 226 us
  waiting for transfers between devices  179 us (79%)
  matrix products  26.1 us (12%)
  between operations  13.4 us (6%)
  other arithmetic  5.89 us (3%)
    reduce_scatter x1, waiting for transfers between devices, shards(): lax.psum_scatter(jnp.dot(activations, down_weight, preferred_element_type...  104 us
    all_gather x1, waiting for transfers between devices, shards(): block_rows = lax.all_gather(normed, 'tensor', axis=0, tiled=True)  75.1 us
    dot_general x1, matrix products, shards(): jnp.dot(activations, down_weight, preferred_element_type=jnp.float32)  18.1 us
    dot_general x1, matrix products, shards(): lax.dot_general(block_rows, gate_weight, dims, preferred_element_type=jnp...  7.95 us
  transfers between devices with their start and end apart: 2, of which 2 were waited for; matrix products, arithmetic and copies ran while one was open for 1% of the time, Pallas kernels for 0%

commit v1 on v0

--- a/solution.py
+++ b/solution.py
@@ -2,6 +2,13 @@
 import jax.numpy as jnp
 from jax import lax
 from jax.sharding import PartitionSpec as P
+
+
+def swapped_in(x, axis, dim):
+    n_dev = lax.axis_size(axis)
+    tiles = jnp.stack([x for _ in range(n_dev)])
+    tiles = lax.all_to_all(tiles, axis, split_axis=0, concat_axis=0)
+    return jnp.concatenate(tiles, axis=dim)
 
 
 def shards(hidden_rows, norm_gain, gate_weight, up_weight, down_weight, span_lengths):
@@ -11,7 +18,7 @@
     scale = lax.rsqrt(jnp.mean(widened * widened, axis=-1, keepdims=True) + 1e-06)
     normed = (widened * scale * norm_gain).astype(jnp.bfloat16)
     dims = (((1,), (1,)), ((), ()))
-    block_rows = lax.all_gather(normed, "tensor", axis=0, tiled=True)
+    block_rows = swapped_in(normed, "tensor", 0)
     gate_part = lax.dot_general(block_rows, gate_weight, dims, preferred_element_type=jnp.float32)
     up_part = lax.dot_general(block_rows, up_weight, dims, preferred_element_type=jnp.float32)
     activations = (jax.nn.silu(gate_part) * up_part).astype(jnp.bfloat16)

time: 226 us -> 242 us (1.071)
  blocking collectives: 0 us -> 91.2 us
  waiting for transfers between devices: 179 us -> 105 us
  local copies, waits for them, and re-layouts: 1.21 us -> 4.85 us
  matrix products: 26.1 us -> 22.6 us
    all_to_all x0 -> x1, blocking collectives: none -> 91.2 us  [swapped_in(): tiles = lax.all_to_all(tiles, axis, split_axis=0, concat_axis=0)]
    all_gather x1 -> x0, waiting for transfers between devices: 75.1 us -> none  [shards(): block_rows = lax.all_gather(normed, 'tensor', axis=0, tiled=True)]
    dot_general x1, matrix products: 7.95 us -> 4.44 us  [shards(): lax.dot_general(block_rows, gate_weight, dims, preferred_element_type=jnp...]
    unnamed x2 -> x6, local copies, waits for them, and re-layouts: 0.63 us -> 3.57 us
  transfers between devices with their start and end apart: 2 -> 1, of which waited for: 2 -> 1; matrix products, arithmetic and copies ran while one was open for 1% -> 1% of each run, Pallas kernels for 0% -> 0%
where the time goes in v1:
time: 242 us
  waiting for transfers between devices  105 us (43%)
  blocking collectives  91.2 us (38%)
  matrix products  22.6 us (9%)
  between operations  13.4 us (6%)
  other arithmetic  5.12 us (2%)
  local copies, waits for them, and re-layouts  4.85 us (2%)
    reduce_scatter x1, waiting for transfers between devices, shards(): lax.psum_scatter(jnp.dot(activations, down_weight, preferred_element_type...  105 us
    all_to_all x1, blocking collectives, swapped_in(): tiles = lax.all_to_all(tiles, axis, split_axis=0, concat_axis=0)  91.2 us
    dot_general x1, matrix products, shards(): jnp.dot(activations, down_weight, preferred_element_type=jnp.float32)  18.1 us
  transfers between devices with their start and end apart: 1, of which 1 were waited for; matrix products, arithmetic and copies ran while one was open for 1% of the time, Pallas kernels for 0%

profile of v1, /device:TPU:1, one launch (start us, length us, event | category | flops | bytes accessed | tf_op | source)
XLA Modules:
  0.0 242.2 jit_solution(14119783468798120413)
XLA Ops:
  6.5 0.0 reduce-scatter.2.cloned.1.call-start
  6.5 1.2 fusion
  7.8 1.2 fusion.2
  9.0 0.7 stack.2
  9.7 0.0 copy-start.1
  9.7 91.2 %all_to_all.5 = bf16[16,64,3584]{2,1,0:T(8,128)(2,1)S(1)} all-to-all(bf16[16,64,3584]{2,1,0:T(8,128)(2,1)S(1)} %stack.2), channel_id=1, replica_groups=mesh['dp'=16,'tensor'=16] {'tensor'}, dimensions={0} | all-to-all | bytes 14680064 | tf_op jit(solution)/shard_map/all_to_all | solution.py:10
  100.9 0.0 copy-start
  100.9 2.9 %copy-done = bf16[16,64,3584]{2,1,0:T(8,128)(2,1)} copy-done((bf16[16,64,3584]{2,1,0:T(8,128)(2,1)}, bf16[16,64,3584]{2,1,0:T(8,128)(2,1)S(1)}, u32[]{:S(2)}) %copy-start) | copy-done | bytes 7340056
  103.8 0.0 copy-done.1
  103.8 4.4 %fusion.3 = f32[1024,576]{0,1:T(8,128)S(1)} fusion(bf16[1024,3584]{1,0:T(8,128)(2,1)S(1)} %bitcast.16, bf16[576,3584]{1,0:T(8,128)(2,1)S(1)} %copy-done.1), kind=kOutput, calls=%fused_computation.9 | convolution fusion | flops 4227858432 | bytes 13828096 | tf_op jit(solution)/shard_map/dot_general | solution.py:22
  108.3 18.1 %fusion.4 = f32[1024,3584]{1,0:T(8,128)} fusion(bf16[576,3584]{1,0:T(8,128)(2,1)} %param.10, f32[1024,576]{0,1:T(8,128)S(1)} %fusion.3, bf16[1024,3584]{1,0:T(8,128)(2,1)} %bitcast.17, bf16[576,3584]{1,0:T(8,128)(2,1)} %param.9), kind=kOutput, calls=%fused_computation.10 | convolution fusion | flops 8459255808 | bytes 32636928 | tf_op jit(solution)/shard_map/dot_general | solution.py:26
  126.4 0.0 copy-start.2
  126.4 0.0 reduce-scatter.2.cloned.1.call-update
  126.4 0.6 copy-done.2
  127.1 0.6 dynamic_slice.3
  127.6 0.6 iota_compare_fusion
  128.3 105.0 %reduce-scatter.2.cloned.1.call-done = f32[64,3584]{1,0:T(8,128)} async-done(((f32[1024,3584]{1,0:T(8,128)}), f32[64,3584]{1,0:T(8,128)}) %reduce-scatter.2.cloned.1.call-update) | async-done | bytes 917520 | tf_op jit(solution)/shard_map/reduce_scatter | solution.py:25
  233.3 2.1 convert_select_fusion
  (1 shorter events, 0.0 us)
Async XLA Ops:
  6.5 226.8 %reduce-scatter.2.cloned.1.call-start = ((), (), s32[]{:S(2)}) async-start(), calls=%async_computation.2 | async-start | bytes 15597568 | tf_op jit(solution)/shard_map/reduce_scatter | solution.py:25
  9.7 94.1 %copy-start.1 = (bf16[576,3584]{1,0:T(8,128)(2,1)S(1)}, bf16[576,3584]{1,0:T(8,128)(2,1)}, u32[]{:S(2)}) copy-start(bf16[576,3584]{1,0:T(8,128)(2,1)} %param.8) | copy-start | bytes 12386308
  100.9 2.9 %copy-start = (bf16[16,64,3584]{2,1,0:T(8,128)(2,1)}, bf16[16,64,3584]{2,1,0:T(8,128)(2,1)S(1)}, u32[]{:S(2)}) copy-start(bf16[16,64,3584]{2,1,0:T(8,128)(2,1)S(1)} %all_to_all.5) | copy-start | bytes 22020100
  126.4 0.7 copy-start.2
Sparse Core Ops, SparseCore 0:
  126.6 106.7 reduce-scatter.1
